TPU v7x, 32 devices: a whole 2x2x4 slice. The times are simulated.
32 devices in a mesh: snp: 8 (over z, y), samp: 4 (over x, core).
Axes of the slice: x: 2, y: 2, z: 4, core: 2. Of those that a mesh axis runs over, the one named last changes fastest.
Arguments:
- genotypes: bfloat16 [1536, 5120], P('samp', 'snp'), may hold values from -0.076171875 to 0.076171875
- responses: float32 [3072, 1536], P('snp', 'samp'), may hold values from -6 to 6
- weights: float32 [1024, 64, 128], P('snp'), may hold values from -6 to 6
- pattern: int32 [1024, 2], P('snp'), may hold values from 0 to 45, as said below
- entry_count: int32 [8], P('snp'), may hold values from 64 to 128, as said below
- tile_slot: int32 [46], replicated, may hold values from 0 to 47, as said below
- penalty: float32 [46], replicated, may hold values from 0.5 to 5
Outputs:
- new_weights: float32 [1024, 64, 128], P('snp')
Inputs may be any that keep to these rules, and one draw needn't show every extreme that they name: `pattern`: column 0 is a block below 5, column 1 a tile below 46; within one segment's 128 rows no (block, tile) pair repeats. `entry_count`: some segment has all 128 entries live. `tile_slot`: distinct slots.
All inputs are finite; a program needn't handle non-finite values.
Results may differ from a plain program's by a relative error of at most 0.0032.
Values may be sent and summed in bfloat16 or wider, within the bound.
No kernel may reach another device: no remote copies, remote signals or barrier semaphores. Data moves between devices by JAX's collectives and lax.ppermute only.
A program may use at most 128 MiB of HBM per device.

v0:
```python
import jax
import jax.numpy as jnp
from jax import lax
from jax.sharding import PartitionSpec as P

ITERS = 2
step_scale = 0.3


def shrink_soft(current, gradient, cutoff, active):
    shifted = current + step_scale * gradient
    shrunk = jnp.sign(shifted) * jnp.maximum(jnp.abs(shifted) - cutoff, jnp.float32(0.0))
    return jnp.where(active[:, None, None], shrunk, jnp.float32(0.0))


def per_device(genotypes, responses, weights, pattern, entry_count, tile_slot, penalty):
    sample_count = genotypes.shape[0]
    entries, tile_width, block_width = weights.shape
    block_count = genotypes.shape[1] // block_width
    own_rows = responses.shape[0]
    owners = lax.axis_size("snp")
    own_slots = own_rows // tile_width
    slot_total = owners * own_slots
    cells = slot_total * block_count
    geno_blocks = genotypes.reshape(sample_count, block_count, block_width)
    blk = pattern[:, 0]
    tile = pattern[:, 1]
    tile_hot = tile[:, None] == jnp.arange(penalty.shape[0], dtype=jnp.int32)[None, :]
    slot_ids = jnp.sum(jnp.where(tile_hot, tile_slot[None, :], 0), axis=1)
    per_entry = jnp.sum(jnp.where(tile_hot, penalty[None, :], jnp.float32(0.0)), axis=1)
    cutoff = step_scale * per_entry[:, None, None]
    cell = slot_ids * block_count + blk
    cell_hot = (cell[:, None] == jnp.arange(cells, dtype=jnp.int32)[None, :]).astype(jnp.bfloat16)
    active = jnp.arange(entries, dtype=jnp.int32) < entry_count[0]
    current = jnp.where(active[:, None, None], weights, jnp.float32(0.0))
    for sweep in range(ITERS):
        weight_bf = current.astype(jnp.bfloat16)
        dense = jnp.einsum(
            "ec,epk->cpk", cell_hot, weight_bf, preferred_element_type=jnp.float32
        ).astype(jnp.bfloat16)
        dense = dense.reshape(slot_total, block_count, tile_width, block_width)
        partial = jnp.einsum(
            "jbpk,sbk->jps", dense, geno_blocks, preferred_element_type=jnp.float32
        ).astype(jnp.bfloat16)
        partial = partial.reshape(owners, own_rows, sample_count)
        gathered = lax.all_to_all(partial, "snp", 0, 0, tiled=False)
        prediction = jnp.sum(gathered.astype(jnp.float32), axis=0)
        residual = (responses - prediction).astype(jnp.bfloat16)
        shard_rows = lax.all_gather(residual, "snp", axis=0, tiled=True)
        blocks = shard_rows.reshape(slot_total, tile_width, sample_count)
        full = jnp.einsum(
            "jps,sbk->jbpk", blocks, geno_blocks, preferred_element_type=jnp.float32
        ).reshape(cells, tile_width, block_width)
        local_gradient = jnp.take(full, cell, axis=0, mode="clip")
        if SPLIT_SAMP:
            part = lax.psum_scatter(local_gradient, "sc", scatter_dimension=0, tiled=True)
            part = lax.psum(part, "sx")
            gradient = lax.all_gather(part, "sc", axis=0, tiled=True)
        else:
            gradient = lax.psum(local_gradient, "samp")
        current = shrink_soft(current, gradient, cutoff, active)
    return current


SPLIT_SAMP = True


def solution(mesh):
    snp_size, samp_size = mesh.devices.shape
    samp = "samp"
    if SPLIT_SAMP:
        devices = mesh.devices.reshape(snp_size, 2, samp_size // 2)
        mesh = jax.sharding.Mesh(devices, ("snp", "sx", "sc"))
        samp = ("sx", "sc")
    in_specs = (
        P(samp, "snp"),
        P("snp", samp),
        P("snp", None, None),
        P("snp", None),
        P("snp"),
        P(),
        P(),
    )
    out_specs = P("snp", None, None)
    return jax.shard_map(
        per_device, mesh=mesh, in_specs=in_specs, out_specs=out_specs, check_vma=False
    )
```

profile of v0, /device:TPU:0, one launch (start us, length us, event | category | flops | bytes accessed | tf_op | source)
XLA Modules:
  0.0 482.6 jit_solution(14898244865369778887)
XLA Ops:
  7.2 0.7 slice_bitcast_fusion
  7.9 0.7 select_reduce_fusion.1
  8.6 0.7 fusion.7
  9.3 1.3 copy.36
  10.6 2.6 select_convert_fusion
  13.2 2.0 convolution_convert_fusion.1
  15.3 1.0 copy.35
  16.3 2.6 bitcast_convert_fusion.1
  18.9 0.0 copy-start
  18.9 61.1 %all_to_all.10 = bf16[8,384,384]{2,1,0:T(8,128)(2,1)S(1)} all-to-all(bf16[8,384,384]{2,1,0:T(8,128)(2,1)S(1)} %bitcast.62), channel_id=1, replica_groups=mesh['snp'=8,'sx'=2,'sc'=2] {'snp'}, dimensions={0} | all-to-all | bytes 4718592 | tf_op jit(solution)/shard_map/all_to_all | solution.py:46
  80.0 0.3 convert_reduce_fusion.1
  80.4 0.8 subtract_convert_fusion.1
  81.2 0.0 all-gather.5.cloned.1.call-update
  81.2 0.0 reduce-scatter.3.cloned.1.call-start
  81.2 51.2 %all-gather.5.cloned.1.call-done = bf16[3072,384]{1,0:T(8,128)(2,1)} async-done(((bf16[384,384]{1,0:T(8,128)(2,1)}), bf16[3072,384]{1,0:T(8,128)(2,1)}) %all-gather.5.cloned.1.call-update) | async-done | bytes 2359312 | tf_op jit(solution)/shard_map/all_gather | solution.py:49
  132.4 7.2 %fusion.9 = f32[48,64,5,128]{3,1,2,0:T(8,128)} fusion(bf16[48,64,384,1]{2,1,3,0:T(8,128)(2,1)} %bitcast.64, bf16[384,5,128,1]{0,2,1,3:T(8,128)(2,1)S(1)} %bitcast.57), kind=kOutput, calls=%fused_computation.29 | convolution fusion | flops 1509949440 | bytes 10715136 | tf_op jit(solution)/shard_map/jps,sbk->jbpk/dot_general | solution.py:51
  139.6 6.1 %gather_fusion = f32[128,64,128]{2,1,0:T(8,128)} fusion(f32[240,64,128]{2,1,0:T(8,128)} %bitcast.55, s32[1024]{0:T(1024)S(1)} %pad_clamp_fusion), kind=kCustom, calls=%fused_computation | custom fusion | bytes 8389120 | tf_op jit(solution)/shard_map/jit(_take)/gather | solution.py:54
  145.7 0.0 reduce-scatter.3.cloned.1.call-update
  145.7 0.0 all-reduce.3.cloned.1.call-start
  145.7 10.7 %reduce-scatter.3.cloned.1.call-done = f32[64,64,128]{2,1,0:T(8,128)} async-done(((f32[128,64,128]{2,1,0:T(8,128)}), f32[64,64,128]{2,1,0:T(8,128)}) %reduce-scatter.3.cloned.1.call-update) | async-done | bytes 2097168 | tf_op jit(solution)/shard_map/reduce_scatter | solution.py:56
  156.4 0.0 all-reduce.3.cloned.1.call-update
  156.4 0.0 all-gather.7.cloned.1.call-start
  156.5 66.6 %all-reduce.3.cloned.1.call-done = f32[64,64,128]{2,1,0:T(8,128)} async-done(((f32[64,64,128]{2,1,0:T(8,128)}), f32[64,64,128]{2,1,0:T(8,128)}) %all-reduce.3.cloned.1.call-update) | async-done | bytes 2097168 | tf_op jit(solution)/shard_map/psum | solution.py:57
  223.0 0.0 all-gather.7.cloned.1.call-update
  223.1 0.2 all-gather.9.cloned.1.call-start
  223.3 0.1 select_reduce_fusion
  223.4 14.7 %all-gather.7.cloned.1.call-done = f32[128,64,128]{2,1,0:T(8,128)} async-done(((f32[64,64,128]{2,1,0:T(8,128)}), f32[128,64,128]{2,1,0:T(8,128)}) %all-gather.7.cloned.1.call-update) | async-done | bytes 4194320 | tf_op jit(solution)/shard_map/all_gather | solution.py:58
  238.1 4.7 fusion.8
  242.9 2.0 convolution_convert_fusion
  244.9 1.0 copy.40
  245.9 2.6 bitcast_convert_fusion
  248.6 59.8 %all_to_all.11 = bf16[8,384,384]{2,1,0:T(8,128)(2,1)S(1)} all-to-all(bf16[8,384,384]{2,1,0:T(8,128)(2,1)S(1)} %bitcast.63), channel_id=1, replica_groups=mesh['snp'=8,'sx'=2,'sc'=2] {'snp'}, dimensions={0} | all-to-all | bytes 4718592 | tf_op jit(solution)/shard_map/all_to_all | solution.py:46
  308.4 0.3 convert_reduce_fusion
  308.7 0.8 subtract_convert_fusion
  309.5 0.0 all-gather.9.cloned.1.call-update
  309.6 0.0 reduce-scatter.5.cloned.1.call-start
  309.6 51.2 %all-gather.9.cloned.1.call-done = bf16[3072,384]{1,0:T(8,128)(2,1)} async-done(((bf16[384,384]{1,0:T(8,128)(2,1)}), bf16[3072,384]{1,0:T(8,128)(2,1)}) %all-gather.9.cloned.1.call-update) | async-done | bytes 2359312 | tf_op jit(solution)/shard_map/all_gather | solution.py:49
  360.8 7.2 %fusion.10 = f32[48,64,5,128]{3,1,2,0:T(8,128)} fusion(bf16[48,64,384,1]{2,1,3,0:T(8,128)(2,1)} %bitcast.65, bf16[384,5,128,1]{0,2,1,3:T(8,128)(2,1)S(1)} %bitcast.59), kind=kOutput, calls=%fused_computation.30 | convolution fusion | flops 1509949440 | bytes 10715136 | tf_op jit(solution)/shard_map/jps,sbk->jbpk/dot_general | solution.py:51
  368.0 6.1 %gather_fusion.1 = f32[128,64,128]{2,1,0:T(8,128)} fusion(f32[240,64,128]{2,1,0:T(8,128)} %bitcast.54, s32[1024]{0:T(1024)S(1)} %pad_clamp_fusion), kind=kCustom, calls=%fused_computation.1 | custom fusion | bytes 8389120 | tf_op jit(solution)/shard_map/jit(_take)/gather | solution.py:54
  374.1 0.0 reduce-scatter.5.cloned.1.call-update
  374.1 0.0 all-reduce.5.cloned.1.call-start
  374.1 10.7 %reduce-scatter.5.cloned.1.call-done = f32[64,64,128]{2,1,0:T(8,128)} async-done(((f32[128,64,128]{2,1,0:T(8,128)}), f32[64,64,128]{2,1,0:T(8,128)}) %reduce-scatter.5.cloned.1.call-update) | async-done | bytes 2097168 | tf_op jit(solution)/shard_map/reduce_scatter | solution.py:56
  384.8 0.0 all-reduce.5.cloned.1.call-update
  384.9 0.0 all-gather.11.cloned.1.call-start
  384.9 66.5 %all-reduce.5.cloned.1.call-done = f32[64,64,128]{2,1,0:T(8,128)} async-done(((f32[64,64,128]{2,1,0:T(8,128)}), f32[64,64,128]{2,1,0:T(8,128)}) %all-reduce.5.cloned.1.call-update) | async-done | bytes 2097168 | tf_op jit(solution)/shard_map/psum | solution.py:57
  451.4 0.0 all-gather.11.cloned.1.call-update
  451.5 15.2 %all-gather.11.cloned.1.call-done = f32[128,64,128]{2,1,0:T(8,128)} async-done(((f32[64,64,128]{2,1,0:T(8,128)}), f32[128,64,128]{2,1,0:T(8,128)}) %all-gather.11.cloned.1.call-update) | async-done | bytes 4194320 | tf_op jit(solution)/shard_map/all_gather | solution.py:58
  466.7 9.1 %multiply_select_fusion = f32[128,64,128]{2,1,0:T(8,128)} fusion(f32[128,64,128]{2,1,0:T(8,128)} %all-gather.11.cloned.1.call-done, f32[128]{0:T(128)S(1)} %broadcast_multiply_fusion, pred[128]{0:T(512)(128)(4,1)S(1)} %iota_compare_fusion.2, f32[128,64,128]{2,1,0:T(8,128)} %all-gather.7.cloned.1.call-done, f32[128,64,128]{2,1,0:T(8,128)} %param.9), kind=kLoop, calls=%fused_computation.6 | loop fusion | flops 17825792 | bytes 16777856 | tf_op jit(solution)/shard_map/jit(_where)/select_n | solution.py:13
  (7 shorter events, 0.0 us)
Async XLA Ops:
  6.5 125.9 %all-gather.5.cloned.1.call-start = ((), (), s32[]{:S(2)}) async-start(), calls=%async_computation.4 | async-start | bytes 2654208 | tf_op jit(solution)/shard_map/all_gather | solution.py:49
  18.9 61.4 %copy-start = (f32[384,384]{1,0:T(8,128)S(1)}, f32[384,384]{1,0:T(8,128)}, u32[]{:S(2)}) copy-start(f32[384,384]{1,0:T(8,128)} %param.8) | copy-start | bytes 1769476
  81.2 75.2 %reduce-scatter.3.cloned.1.call-start = ((), (), s32[]{:S(2)}) async-start(), calls=%async_computation.5 | async-start | bytes 6291456 | tf_op jit(solution)/shard_map/reduce_scatter | solution.py:56
  145.6 77.6 %copy-start.1 = (f32[46]{0:T(128)S(1)}, f32[46]{0:T(128)}, u32[]{:S(2)}) copy-start(f32[46]{0:T(128)} %param.13) | copy-start | bytes 556
  145.7 77.4 %all-reduce.3.cloned.1.call-start = ((), (), s32[]{:S(2)}) async-start(), calls=%async_computation.6 | async-start | bytes 4194304 | tf_op jit(solution)/shard_map/psum | solution.py:57
  156.4 81.7 %all-gather.7.cloned.1.call-start = ((), (), s32[]{:S(2)}) async-start(), calls=%async_computation.7 | async-start | bytes 6291456 | tf_op jit(solution)/shard_map/all_gather | solution.py:58
  223.1 137.8 %all-gather.9.cloned.1.call-start = ((), (), s32[]{:S(2)}) async-start(), calls=%async_computation.8 | async-start | bytes 2654208 | tf_op jit(solution)/shard_map/all_gather | solution.py:49
  309.6 75.3 %reduce-scatter.5.cloned.1.call-start = ((), (), s32[]{:S(2)}) async-start(), calls=%async_computation.9 | async-start | bytes 6291456 | tf_op jit(solution)/shard_map/reduce_scatter | solution.py:56
  374.1 77.3 %all-reduce.5.cloned.1.call-start = ((), (), s32[]{:S(2)}) async-start(), calls=%async_computation.10 | async-start | bytes 4194304 | tf_op jit(solution)/shard_map/psum | solution.py:57
  384.9 81.8 %all-gather.11.cloned.1.call-start = ((), (), s32[]{:S(2)}) async-start(), calls=%async_computation.11 | async-start | bytes 6291456 | tf_op jit(solution)/shard_map/all_gather | solution.py:58
Sparse Core Ops, SparseCore 0:
  81.3 51.0 all-gather.4
  145.8 10.5 reduce-scatter.2
  158.8 64.1 all-reduce.2
  224.4 13.6 all-gather.6
  309.7 51.1 all-gather.8
  374.2 10.5 reduce-scatter.4
  387.2 64.1 all-reduce.4
  453.0 13.6 all-gather.10
where the time goes:
time: 483 us
  waiting for transfers between devices  287 us (59%)
  blocking collectives  121 us (25%)
  matrix products  23.6 us (5%)
  other arithmetic  20.2 us (4%)
  local copies, waits for them, and re-layouts  16.1 us (3%)
  between operations  14.3 us (3%)
    psum x2, waiting for transfers between devices, per_device(): part = lax.psum(part, 'sx')  133 us
    all_to_all x2, blocking collectives, per_device(): gathered = lax.all_to_all(partial, 'snp', 0, 0, tiled=False)  121 us
    all_gather x2, waiting for transfers between devices, per_device(): shard_rows = lax.all_gather(residual, 'snp', axis=0, tiled=True)  102 us
    all_gather x2, waiting for transfers between devices, per_device(): gradient = lax.all_gather(part, 'sc', axis=0, tiled=True)  30 us
    reduce_scatter x2, waiting for transfers between devices, per_device(): lax.psum_scatter(local_gradient, 'sc', scatter_dimension=0, tiled=True)  21.4 us
    dot_general x2, matrix products, per_device(): jnp.einsum('jps,sbk->jbpk', blocks, geno_blocks, preferred_element_type=j...  14.3 us
    gather x2, local copies, waits for them, and re-layouts, per_device(): local_gradient = jnp.take(full, cell, axis=0, mode='clip')  12.1 us
  transfers between devices with their start and end apart: 8, of which 8 were waited for; matrix products, arithmetic and copies ran while one was open for 0% of the time, Pallas kernels for 0%

commit v1 on v0

--- a/solution.py
+++ b/solution.py
@@ -46,7 +46,14 @@
         gathered = lax.all_to_all(partial, "snp", 0, 0, tiled=False)
         prediction = jnp.sum(gathered.astype(jnp.float32), axis=0)
         residual = (responses - prediction).astype(jnp.bfloat16)
-        shard_rows = lax.all_gather(residual, "snp", axis=0, tiled=True)
+        ring = [residual]
+        for hop in range(7):
+            ring.append(lax.ppermute(ring[-1], "snp", [(dev, (dev + 1) % 8) for dev in range(8)]))
+        shard_rows = jnp.roll(
+            jnp.concatenate(ring[::-1], axis=0),
+            (lax.axis_index("snp") + 1) * ring[0].shape[0],
+            axis=0,
+        )
         blocks = shard_rows.reshape(slot_total, tile_width, sample_count)
         full = jnp.einsum(
             "jps,sbk->jbpk", blocks, geno_blocks, preferred_element_type=jnp.float32

time: 483 us -> 525 us (1.087)
  waiting for transfers between devices: 287 us -> 320 us
  other arithmetic: 20.2 us -> 29.8 us
    ppermute x0 -> x14, waiting for transfers between devices: none -> 139 us  [per_device(): lax.ppermute(ring[-1], 'snp', [(dev, (dev + 1) % 8) for dev in range(8)])]
    all_gather x2 -> x0, waiting for transfers between devices: 102 us -> none  [per_device(): shard_rows = lax.all_gather(residual, 'snp', axis=0, tiled=True)]
    concatenate x0 -> x2, other arithmetic: none -> 10.9 us  [per_device(): jnp.roll(jnp.concatenate(ring[::-1], axis=0), (lax.axis_index('snp') + 1)...]
  transfers between devices with their start and end apart: 8 -> 20, of which waited for: 8 -> 20; matrix products, arithmetic and copies ran while one was open for 0% -> 0% of each run, Pallas kernels for 0% -> 0%
where the time goes in v1:
time: 525 us
  waiting for transfers between devices  320 us (61%)
  blocking collectives  121 us (23%)
  other arithmetic  29.8 us (6%)
  matrix products  18.4 us (4%)
  local copies, waits for them, and re-layouts  17.6 us (3%)
  between operations  14.4 us (3%)
    ppermute x14, waiting for transfers between devices, per_device(): lax.ppermute(ring[-1], 'snp', [(dev, (dev + 1) % 8) for dev in range(8)])  139 us
    psum x2, waiting for transfers between devices, per_device(): part = lax.psum(part, 'sx')  133 us
    all_to_all x2, blocking collectives, per_device(): gathered = lax.all_to_all(partial, 'snp', 0, 0, tiled=False)  121 us
    all_gather x2, waiting for transfers between devices, per_device(): gradient = lax.all_gather(part, 'sc', axis=0, tiled=True)  29.9 us
    reduce_scatter x2, waiting for transfers between devices, per_device(): lax.psum_scatter(local_gradient, 'sc', scatter_dimension=0, tiled=True)  18.8 us
    gather x2, local copies, waits for them, and re-layouts, per_device(): local_gradient = jnp.take(full, cell, axis=0, mode='clip')  12.1 us
    concatenate x2, other arithmetic, per_device(): jnp.roll(jnp.concatenate(ring[::-1], axis=0), (lax.axis_index('snp') + 1)...  10.9 us
  transfers between devices with their start and end apart: 20, of which 20 were waited for; matrix products, arithmetic and copies ran while one was open for 0% of the time, Pallas kernels for 0%

profile of v1, /device:TPU:0, one launch (start us, length us, event | category | flops | bytes accessed | tf_op | source)
XLA Modules:
  0.0 524.7 jit_solution(5346652362206630392)
XLA Ops:
  7.2 0.7 slice_bitcast_fusion
  7.9 0.7 select_reduce_fusion.1
  8.6 0.7 fusion.9
  9.3 1.3 copy.36
  10.6 2.6 select_convert_fusion
  13.2 2.0 convolution_convert_fusion.1
  15.3 1.0 copy.35
  16.3 2.6 bitcast_convert_fusion.1
  18.9 60.9 %all_to_all.10 = bf16[8,384,384]{2,1,0:T(8,128)(2,1)S(1)} all-to-all(bf16[8,384,384]{2,1,0:T(8,128)(2,1)S(1)} %bitcast.64), channel_id=1, replica_groups=mesh['snp'=8,'sx'=2,'sc'=2] {'snp'}, dimensions={0} | all-to-all | bytes 4718592 | tf_op jit(solution)/shard_map/all_to_all | solution.py:46
  79.9 0.3 convert_reduce_fusion.1
  80.2 0.7 copy-done
  81.0 1.5 collective-permute-start
  82.5 8.9 %collective-permute-done = bf16[384,384]{1,0:T(8,128)(2,1)S(1)} collective-permute-done((bf16[384,384]{1,0:T(8,128)(2,1)S(1)}, bf16[384,384]{1,0:T(8,128)(2,1)S(1)}, u32[]{:S(2)}, u32[]{:S(2)}) %collective-permute-start) | collective-permute-done | bytes 294944 | tf_op jit(solution)/shard_map/ppermute | solution.py:51
  91.4 9.4 %collective-permute-done.1 = bf16[384,384]{1,0:T(8,128)(2,1)S(1)} collective-permute-done((bf16[384,384]{1,0:T(8,128)(2,1)S(1)}, bf16[384,384]{1,0:T(8,128)(2,1)S(1)}, u32[]{:S(2)}, u32[]{:S(2)}) %collective-permute-start.1) | collective-permute-done | bytes 294944 | tf_op jit(solution)/shard_map/ppermute | solution.py:51
  100.8 9.4 %collective-permute-done.2 = bf16[384,384]{1,0:T(8,128)(2,1)S(1)} collective-permute-done((bf16[384,384]{1,0:T(8,128)(2,1)S(1)}, bf16[384,384]{1,0:T(8,128)(2,1)S(1)}, u32[]{:S(2)}, u32[]{:S(2)}) %collective-permute-start.2) | collective-permute-done | bytes 294944 | tf_op jit(solution)/shard_map/ppermute | solution.py:51
  110.2 9.7 %collective-permute-done.3 = bf16[384,384]{1,0:T(8,128)(2,1)S(1)} collective-permute-done((bf16[384,384]{1,0:T(8,128)(2,1)S(1)}, bf16[384,384]{1,0:T(8,128)(2,1)S(1)}, u32[]{:S(2)}, u32[]{:S(2)}) %collective-permute-start.3) | collective-permute-done | bytes 294944 | tf_op jit(solution)/shard_map/ppermute | solution.py:51
  120.0 10.8 %collective-permute-done.4 = bf16[384,384]{1,0:T(8,128)(2,1)S(1)} collective-permute-done((bf16[384,384]{1,0:T(8,128)(2,1)S(1)}, bf16[384,384]{1,0:T(8,128)(2,1)S(1)}, u32[]{:S(2)}, u32[]{:S(2)}) %collective-permute-start.4) | collective-permute-done | bytes 294944 | tf_op jit(solution)/shard_map/ppermute | solution.py:51
  130.8 12.0 %collective-permute-done.5 = bf16[384,384]{1,0:T(8,128)(2,1)S(1)} collective-permute-done((bf16[384,384]{1,0:T(8,128)(2,1)S(1)}, bf16[384,384]{1,0:T(8,128)(2,1)S(1)}, u32[]{:S(2)}, u32[]{:S(2)}) %collective-permute-start.5) | collective-permute-done | bytes 294944 | tf_op jit(solution)/shard_map/ppermute | solution.py:51
  142.8 9.4 %collective-permute-done.6 = bf16[384,384]{1,0:T(8,128)(2,1)S(1)} collective-permute-done((bf16[384,384]{1,0:T(8,128)(2,1)S(1)}, bf16[384,384]{1,0:T(8,128)(2,1)S(1)}, u32[]{:S(2)}, u32[]{:S(2)}) %collective-permute-start.6) | collective-permute-done | bytes 294944 | tf_op jit(solution)/shard_map/ppermute | solution.py:51
  152.6 5.5 %fusion.1 = bf16[3072,384]{1,0:T(8,128)(2,1)S(1)} fusion(s32[]{:T(128)S(6)} %select_n.36, bf16[3072,384]{1,0:T(8,128)(2,1)S(1)} %constant_dynamic-update-slice_fusion), kind=kLoop, calls=%fused_computation.16 | loop fusion | flops 4718592 | bytes 4718596 | tf_op jit(solution)/shard_map/jit(_roll_dynamic)/concatenate | solution.py:52
  158.1 4.6 fusion.11
  162.7 6.1 %gather_fusion = f32[128,64,128]{2,1,0:T(8,128)} fusion(f32[240,64,128]{2,1,0:T(8,128)} %bitcast.55, s32[1024]{0:T(1024)S(1)} %pad_clamp_fusion), kind=kCustom, calls=%fused_computation | custom fusion | bytes 8389120 | tf_op jit(solution)/shard_map/jit(_take)/gather | solution.py:61
  168.8 9.4 %reduce-scatter.3.cloned.1.call-done = f32[64,64,128]{2,1,0:T(8,128)} async-done(((f32[128,64,128]{2,1,0:T(8,128)}), f32[64,64,128]{2,1,0:T(8,128)}) %reduce-scatter.3.cloned.1.call-update) | async-done | bytes 2097168 | tf_op jit(solution)/shard_map/reduce_scatter | solution.py:63
  178.3 66.6 %all-reduce.3.cloned.1.call-done = f32[64,64,128]{2,1,0:T(8,128)} async-done(((f32[64,64,128]{2,1,0:T(8,128)}), f32[64,64,128]{2,1,0:T(8,128)}) %all-reduce.3.cloned.1.call-update) | async-done | bytes 2097168 | tf_op jit(solution)/shard_map/psum | solution.py:64
  244.9 0.3 reduce-scatter.5.cloned.1.call-start
  245.1 0.1 select_reduce_fusion
  245.2 14.9 %all-gather.3.cloned.1.call-done = f32[128,64,128]{2,1,0:T(8,128)} async-done(((f32[64,64,128]{2,1,0:T(8,128)}), f32[128,64,128]{2,1,0:T(8,128)}) %all-gather.3.cloned.1.call-update) | async-done | bytes 4194320 | tf_op jit(solution)/shard_map/all_gather | solution.py:65
  260.1 4.7 fusion.10
  264.8 2.0 convolution_convert_fusion
  266.9 1.0 copy.40
  267.9 2.6 bitcast_convert_fusion
  270.5 59.8 %all_to_all.11 = bf16[8,384,384]{2,1,0:T(8,128)(2,1)S(1)} all-to-all(bf16[8,384,384]{2,1,0:T(8,128)(2,1)S(1)} %bitcast.65), channel_id=1, replica_groups=mesh['snp'=8,'sx'=2,'sc'=2] {'snp'}, dimensions={0} | all-to-all | bytes 4718592 | tf_op jit(solution)/shard_map/all_to_all | solution.py:46
  330.4 0.3 convert_reduce_fusion
  330.8 1.5 collective-permute-start.7
  332.3 9.3 %collective-permute-done.7 = bf16[384,384]{1,0:T(8,128)(2,1)S(1)} collective-permute-done((bf16[384,384]{1,0:T(8,128)(2,1)S(1)}, bf16[384,384]{1,0:T(8,128)(2,1)S(1)}, u32[]{:S(2)}, u32[]{:S(2)}) %collective-permute-start.7) | collective-permute-done | bytes 294944 | tf_op jit(solution)/shard_map/ppermute | solution.py:51
  341.6 9.9 %collective-permute-done.8 = bf16[384,384]{1,0:T(8,128)(2,1)S(1)} collective-permute-done((bf16[384,384]{1,0:T(8,128)(2,1)S(1)}, bf16[384,384]{1,0:T(8,128)(2,1)S(1)}, u32[]{:S(2)}, u32[]{:S(2)}) %collective-permute-start.8) | collective-permute-done | bytes 294944 | tf_op jit(solution)/shard_map/ppermute | solution.py:51
  351.5 9.4 %collective-permute-done.9 = bf16[384,384]{1,0:T(8,128)(2,1)S(1)} collective-permute-done((bf16[384,384]{1,0:T(8,128)(2,1)S(1)}, bf16[384,384]{1,0:T(8,128)(2,1)S(1)}, u32[]{:S(2)}, u32[]{:S(2)}) %collective-permute-start.9) | collective-permute-done | bytes 294944 | tf_op jit(solution)/shard_map/ppermute | solution.py:51
  360.9 9.4 %collective-permute-done.10 = bf16[384,384]{1,0:T(8,128)(2,1)S(1)} collective-permute-done((bf16[384,384]{1,0:T(8,128)(2,1)S(1)}, bf16[384,384]{1,0:T(8,128)(2,1)S(1)}, u32[]{:S(2)}, u32[]{:S(2)}) %collective-permute-start.10) | collective-permute-done | bytes 294944 | tf_op jit(solution)/shard_map/ppermute | solution.py:51
  370.3 10.2 %collective-permute-done.11 = bf16[384,384]{1,0:T(8,128)(2,1)S(1)} collective-permute-done((bf16[384,384]{1,0:T(8,128)(2,1)S(1)}, bf16[384,384]{1,0:T(8,128)(2,1)S(1)}, u32[]{:S(2)}, u32[]{:S(2)}) %collective-permute-start.11) | collective-permute-done | bytes 294944 | tf_op jit(solution)/shard_map/ppermute | solution.py:51
  380.5 11.3 %collective-permute-done.12 = bf16[384,384]{1,0:T(8,128)(2,1)S(1)} collective-permute-done((bf16[384,384]{1,0:T(8,128)(2,1)S(1)}, bf16[384,384]{1,0:T(8,128)(2,1)S(1)}, u32[]{:S(2)}, u32[]{:S(2)}) %collective-permute-start.12) | collective-permute-done | bytes 294944 | tf_op jit(solution)/shard_map/ppermute | solution.py:51
  391.8 9.4 %collective-permute-done.13 = bf16[384,384]{1,0:T(8,128)(2,1)S(1)} collective-permute-done((bf16[384,384]{1,0:T(8,128)(2,1)S(1)}, bf16[384,384]{1,0:T(8,128)(2,1)S(1)}, u32[]{:S(2)}, u32[]{:S(2)}) %collective-permute-start.13) | collective-permute-done | bytes 294944 | tf_op jit(solution)/shard_map/ppermute | solution.py:51
  401.7 5.5 %fusion = bf16[3072,384]{1,0:T(8,128)(2,1)S(1)} fusion(s32[]{:T(128)S(6)} %select_n.36, bf16[3072,384]{1,0:T(8,128)(2,1)S(1)} %constant_dynamic-update-slice_fusion.8), kind=kLoop, calls=%fused_computation.15 | loop fusion | flops 4718592 | bytes 4718596 | tf_op jit(solution)/shard_map/jit(_roll_dynamic)/concatenate | solution.py:52
  407.1 4.5 fusion.12
  411.7 6.1 %gather_fusion.1 = f32[128,64,128]{2,1,0:T(8,128)} fusion(f32[240,64,128]{2,1,0:T(8,128)} %bitcast.54, s32[1024]{0:T(1024)S(1)} %pad_clamp_fusion), kind=kCustom, calls=%fused_computation.1 | custom fusion | bytes 8389120 | tf_op jit(solution)/shard_map/jit(_take)/gather | solution.py:61
  417.8 9.4 %reduce-scatter.5.cloned.1.call-done = f32[64,64,128]{2,1,0:T(8,128)} async-done(((f32[128,64,128]{2,1,0:T(8,128)}), f32[64,64,128]{2,1,0:T(8,128)}) %reduce-scatter.5.cloned.1.call-update) | async-done | bytes 2097168 | tf_op jit(solution)/shard_map/reduce_scatter | solution.py:63
  427.3 66.4 %all-reduce.5.cloned.1.call-done = f32[64,64,128]{2,1,0:T(8,128)} async-done(((f32[64,64,128]{2,1,0:T(8,128)}), f32[64,64,128]{2,1,0:T(8,128)}) %all-reduce.5.cloned.1.call-update) | async-done | bytes 2097168 | tf_op jit(solution)/shard_map/psum | solution.py:64
  493.7 15.1 %all-gather.5.cloned.1.call-done = f32[128,64,128]{2,1,0:T(8,128)} async-done(((f32[64,64,128]{2,1,0:T(8,128)}), f32[128,64,128]{2,1,0:T(8,128)}) %all-gather.5.cloned.1.call-update) | async-done | bytes 4194320 | tf_op jit(solution)/shard_map/all_gather | solution.py:65
  508.8 9.1 %multiply_select_fusion = f32[128,64,128]{2,1,0:T(8,128)} fusion(f32[128,64,128]{2,1,0:T(8,128)} %all-gather.5.cloned.1.call-done, f32[128]{0:T(128)S(1)} %broadcast_multiply_fusion, pred[128]{0:T(512)(128)(4,1)S(1)} %iota_compare_fusion.2, f32[128,64,128]{2,1,0:T(8,128)} %all-gather.3.cloned.1.call-done, f32[128,64,128]{2,1,0:T(8,128)} %param.11), kind=kLoop, calls=%fused_computation.10 | loop fusion | flops 17825792 | bytes 16777856 | tf_op jit(solution)/shard_map/jit(_where)/select_n | solution.py:13
  (47 shorter events, 1.2 us)
Async XLA Ops:
  6.5 171.7 %reduce-scatter.3.cloned.1.call-start = ((), (), s32[]{:S(2)}) async-start(), calls=%async_computation.4 | async-start | bytes 6291456 | tf_op jit(solution)/shard_map/reduce_scatter | solution.py:63
  79.9 1.1 copy-start
  81.0 10.4 %collective-permute-start = (bf16[384,384]{1,0:T(8,128)(2,1)S(1)}, bf16[384,384]{1,0:T(8,128)(2,1)S(1)}, u32[]{:S(2)}, u32[]{:S(2)}) collective-permute-start(bf16[384,384]{1,0:T(8,128)(2,1)S(1)} %subtract_convert_fusion.1), channel_id=1, source_target_pairs={{0,4},{4,8},{8,12},{12,16},{16,20},{20,24},{24,28},{28,0},{1,5},{5... | collective-permute-start | bytes 884744 | tf_op jit(solution)/shard_map/ppermute | solution.py:51
  91.4 9.4 %collective-permute-start.1 = (bf16[384,384]{1,0:T(8,128)(2,1)S(1)}, bf16[384,384]{1,0:T(8,128)(2,1)S(1)}, u32[]{:S(2)}, u32[]{:S(2)}) collective-permute-start(bf16[384,384]{1,0:T(8,128)(2,1)S(1)} %collective-permute-done), channel_id=1, source_target_pairs={{0,4},{4,8},{8,12},{12,16},{16,20},{20,24},{24,28},{28,0},{1,5},{5... | collective-permute-start | bytes 884744 | tf_op jit(solution)/shard_map/ppermute | solution.py:51
  100.8 9.4 %collective-permute-start.2 = (bf16[384,384]{1,0:T(8,128)(2,1)S(1)}, bf16[384,384]{1,0:T(8,128)(2,1)S(1)}, u32[]{:S(2)}, u32[]{:S(2)}) collective-permute-start(bf16[384,384]{1,0:T(8,128)(2,1)S(1)} %collective-permute-done.1), channel_id=1, source_target_pairs={{0,4},{4,8},{8,12},{12,16},{16,20},{20,24},{24,28},{28,0},{1,5},{5... | collective-permute-start | bytes 884744 | tf_op jit(solution)/shard_map/ppermute | solution.py:51
  110.2 9.7 %collective-permute-start.3 = (bf16[384,384]{1,0:T(8,128)(2,1)S(1)}, bf16[384,384]{1,0:T(8,128)(2,1)S(1)}, u32[]{:S(2)}, u32[]{:S(2)}) collective-permute-start(bf16[384,384]{1,0:T(8,128)(2,1)S(1)} %collective-permute-done.2), channel_id=1, source_target_pairs={{0,4},{4,8},{8,12},{12,16},{16,20},{20,24},{24,28},{28,0},{1,5},{5... | collective-permute-start | bytes 884744 | tf_op jit(solution)/shard_map/ppermute | solution.py:51
  120.0 10.8 %collective-permute-start.4 = (bf16[384,384]{1,0:T(8,128)(2,1)S(1)}, bf16[384,384]{1,0:T(8,128)(2,1)S(1)}, u32[]{:S(2)}, u32[]{:S(2)}) collective-permute-start(bf16[384,384]{1,0:T(8,128)(2,1)S(1)} %collective-permute-done.3), channel_id=1, source_target_pairs={{0,4},{4,8},{8,12},{12,16},{16,20},{20,24},{24,28},{28,0},{1,5},{5... | collective-permute-start | bytes 884744 | tf_op jit(solution)/shard_map/ppermute | solution.py:51
  130.8 12.0 %collective-permute-start.5 = (bf16[384,384]{1,0:T(8,128)(2,1)S(1)}, bf16[384,384]{1,0:T(8,128)(2,1)S(1)}, u32[]{:S(2)}, u32[]{:S(2)}) collective-permute-start(bf16[384,384]{1,0:T(8,128)(2,1)S(1)} %collective-permute-done.4), channel_id=1, source_target_pairs={{0,4},{4,8},{8,12},{12,16},{16,20},{20,24},{24,28},{28,0},{1,5},{5... | collective-permute-start | bytes 884744 | tf_op jit(solution)/shard_map/ppermute | solution.py:51
  142.8 9.4 %collective-permute-start.6 = (bf16[384,384]{1,0:T(8,128)(2,1)S(1)}, bf16[384,384]{1,0:T(8,128)(2,1)S(1)}, u32[]{:S(2)}, u32[]{:S(2)}) collective-permute-start(bf16[384,384]{1,0:T(8,128)(2,1)S(1)} %collective-permute-done.5), channel_id=1, source_target_pairs={{0,4},{4,8},{8,12},{12,16},{16,20},{20,24},{24,28},{28,0},{1,5},{5... | collective-permute-start | bytes 884744 | tf_op jit(solution)/shard_map/ppermute | solution.py:51
  168.7 76.4 %copy-start.1 = (f32[46]{0:T(128)S(1)}, f32[46]{0:T(128)}, u32[]{:S(2)}) copy-start(f32[46]{0:T(128)} %param.15) | copy-start | bytes 556
  168.8 76.1 %all-reduce.3.cloned.1.call-start = ((), (), s32[]{:S(2)}) async-start(), calls=%async_computation.5 | async-start | bytes 4194304 | tf_op jit(solution)/shard_map/psum | solution.py:64
  178.2 81.9 %all-gather.3.cloned.1.call-start = ((), (), s32[]{:S(2)}) async-start(), calls=%async_computation.6 | async-start | bytes 6291456 | tf_op jit(solution)/shard_map/all_gather | solution.py:65
  244.9 182.4 %reduce-scatter.5.cloned.1.call-start = ((), (), s32[]{:S(2)}) async-start(), calls=%async_computation.7 | async-start | bytes 6291456 | tf_op jit(solution)/shard_map/reduce_scatter | solution.py:63
  330.8 10.8 %collective-permute-start.7 = (bf16[384,384]{1,0:T(8,128)(2,1)S(1)}, bf16[384,384]{1,0:T(8,128)(2,1)S(1)}, u32[]{:S(2)}, u32[]{:S(2)}) collective-permute-start(bf16[384,384]{1,0:T(8,128)(2,1)S(1)} %subtract_convert_fusion), channel_id=1, source_target_pairs={{0,4},{4,8},{8,12},{12,16},{16,20},{20,24},{24,28},{28,0},{1,5},{5... | collective-permute-start | bytes 884744 | tf_op jit(solution)/shard_map/ppermute | solution.py:51
  341.6 9.9 %collective-permute-start.8 = (bf16[384,384]{1,0:T(8,128)(2,1)S(1)}, bf16[384,384]{1,0:T(8,128)(2,1)S(1)}, u32[]{:S(2)}, u32[]{:S(2)}) collective-permute-start(bf16[384,384]{1,0:T(8,128)(2,1)S(1)} %collective-permute-done.7), channel_id=1, source_target_pairs={{0,4},{4,8},{8,12},{12,16},{16,20},{20,24},{24,28},{28,0},{1,5},{5... | collective-permute-start | bytes 884744 | tf_op jit(solution)/shard_map/ppermute | solution.py:51
  351.5 9.4 %collective-permute-start.9 = (bf16[384,384]{1,0:T(8,128)(2,1)S(1)}, bf16[384,384]{1,0:T(8,128)(2,1)S(1)}, u32[]{:S(2)}, u32[]{:S(2)}) collective-permute-start(bf16[384,384]{1,0:T(8,128)(2,1)S(1)} %collective-permute-done.8), channel_id=1, source_target_pairs={{0,4},{4,8},{8,12},{12,16},{16,20},{20,24},{24,28},{28,0},{1,5},{5... | collective-permute-start | bytes 884744 | tf_op jit(solution)/shard_map/ppermute | solution.py:51
  360.9 9.4 %collective-permute-start.10 = (bf16[384,384]{1,0:T(8,128)(2,1)S(1)}, bf16[384,384]{1,0:T(8,128)(2,1)S(1)}, u32[]{:S(2)}, u32[]{:S(2)}) collective-permute-start(bf16[384,384]{1,0:T(8,128)(2,1)S(1)} %collective-permute-done.9), channel_id=1, source_target_pairs={{0,4},{4,8},{8,12},{12,16},{16,20},{20,24},{24,28},{28,0},{1,5},{5... | collective-permute-start | bytes 884744 | tf_op jit(solution)/shard_map/ppermute | solution.py:51
  370.3 10.2 %collective-permute-start.11 = (bf16[384,384]{1,0:T(8,128)(2,1)S(1)}, bf16[384,384]{1,0:T(8,128)(2,1)S(1)}, u32[]{:S(2)}, u32[]{:S(2)}) collective-permute-start(bf16[384,384]{1,0:T(8,128)(2,1)S(1)} %collective-permute-done.10), channel_id=1, source_target_pairs={{0,4},{4,8},{8,12},{12,16},{16,20},{20,24},{24,28},{28,0},{1,5},{5... | collective-permute-start | bytes 884744 | tf_op jit(solution)/shard_map/ppermute | solution.py:51
  380.5 11.3 %collective-permute-start.12 = (bf16[384,384]{1,0:T(8,128)(2,1)S(1)}, bf16[384,384]{1,0:T(8,128)(2,1)S(1)}, u32[]{:S(2)}, u32[]{:S(2)}) collective-permute-start(bf16[384,384]{1,0:T(8,128)(2,1)S(1)} %collective-permute-done.11), channel_id=1, source_target_pairs={{0,4},{4,8},{8,12},{12,16},{16,20},{20,24},{24,28},{28,0},{1,5},{5... | collective-permute-start | bytes 884744 | tf_op jit(solution)/shard_map/ppermute | solution.py:51
  391.8 9.4 %collective-permute-start.13 = (bf16[384,384]{1,0:T(8,128)(2,1)S(1)}, bf16[384,384]{1,0:T(8,128)(2,1)S(1)}, u32[]{:S(2)}, u32[]{:S(2)}) collective-permute-start(bf16[384,384]{1,0:T(8,128)(2,1)S(1)} %collective-permute-done.12), channel_id=1, source_target_pairs={{0,4},{4,8},{8,12},{12,16},{16,20},{20,24},{24,28},{28,0},{1,5},{5... | collective-permute-start | bytes 884744 | tf_op jit(solution)/shard_map/ppermute | solution.py:51
  417.8 75.9 %all-reduce.5.cloned.1.call-start = ((), (), s32[]{:S(2)}) async-start(), calls=%async_computation.8 | async-start | bytes 4194304 | tf_op jit(solution)/shard_map/psum | solution.py:64
  427.3 81.5 %all-gather.5.cloned.1.call-start = ((), (), s32[]{:S(2)}) async-start(), calls=%async_computation.9 | async-start | bytes 6291456 | tf_op jit(solution)/shard_map/all_gather | solution.py:65
Sparse Core Ops, SparseCore 0:
  168.9 9.2 reduce-scatter.2
  180.6 64.2 all-reduce.2
  246.4 13.6 all-gather.2
  417.9 9.2 reduce-scatter.4
  429.5 64.1 all-reduce.4
  495.1 13.6 all-gather.4
